TPU v7x, 512 devices: a whole 4x4x16 slice. The times are simulated.
512 devices in a mesh: req: 128 (over z, x, core), head: 4 (over y).
Axes of the slice: x: 4, y: 4, z: 16, core: 2. Of those that a mesh axis runs over, the one named last changes fastest.
Arguments:
- query_proj: bfloat16 [32768, 2048], P('req', 'head'), may hold values from -6 to 6
- key_proj: bfloat16 [32768, 2048], P('req', 'head'), may hold values from -6 to 6
- value_proj: bfloat16 [32768, 2048], P('req', 'head'), may hold values from -6 to 6
- lengths: int32 [64], replicated, may hold values from 1 to 8, 256 in all
- page_table: int32 [256], P('req'), may hold values from 0 to 255, as said below
- out_weight: bfloat16 [2048, 4096], P('req', 'head'), may hold values from -0.125 to 0.125
- out_bias: float32 [4096], P('head'), may hold values from -3 to 3
Outputs:
- attended: bfloat16 [32768, 4096], P('req', 'head')
- kv_pages: bfloat16 [256, 2, 128, 2048], P('req', None, None, 'head')
Inputs may be any that keep to these rules, and one draw needn't show every extreme that they name: page_table is a permutation in which page b of the stream goes to one of the pages 2 * (b // 2) to 2 * (b // 2) + 1.
All inputs are finite; a program needn't handle non-finite values.
Results may differ from a plain program's by a relative error of at most 0.0046.
Values may be sent and summed in bfloat16 or wider, within the bound.
No kernel may reach another device: no remote copies, remote signals or barrier semaphores. Data moves between devices by JAX's collectives and lax.ppermute only.
A program may use at most 64 MiB of HBM per device.

v0:
```python
import math
import jax
import jax.numpy as jnp
from jax import lax
from jax.sharding import Mesh, PartitionSpec as P

DH = 128
ROT = 32
PAGE = 128
BLK_DEV = 2
REACH = 4
TOK_DEV = 256
rope_base = 10000.0
REQ = ("z", "x", "core")


def passed_along(array, axis, by):
    count = lax.axis_size(axis)
    pairs = [(i, i + by) for i in range(count) if 0 <= i + by < count]
    return lax.ppermute(array, axis, pairs)


def request_info(lengths, token_index):
    request_ends = jnp.cumsum(lengths) * PAGE
    request_starts = request_ends - lengths * PAGE
    inside = request_starts[None, :] <= token_index[:, None]
    request_id = jnp.sum(inside.astype(jnp.int32), axis=1) - 1
    opening = jnp.max(jnp.where(inside, request_starts[None, :], 0), axis=1)
    return (request_id, token_index - opening)


def rotate_heads(projected, position):
    values_f32 = projected.astype(jnp.float32)
    half_rot = ROT // 2
    frequency = jnp.exp(
        jnp.arange(half_rot, dtype=jnp.float32) * (-2.0 * math.log(rope_base) / ROT)
    )
    angles = position.astype(jnp.float32)[:, None] * frequency[None, :]
    cosine = jnp.cos(angles)[:, None, :]
    sine = jnp.sin(angles)[:, None, :]
    front_half = values_f32[..., :half_rot]
    back_half = values_f32[..., half_rot:ROT]
    turned = jnp.concatenate(
        [
            front_half * cosine - back_half * sine,
            back_half * cosine + front_half * sine,
            values_f32[..., ROT:],
        ],
        axis=-1,
    )
    return turned.astype(jnp.bfloat16)


def attend_block(query_rot, key_rot, value_rows, query_id, query_token, key_id, key_token):
    scores = jnp.einsum("qhd,khd->hqk", query_rot, key_rot, preferred_element_type=jnp.float32) * (
        1.0 / math.sqrt(DH)
    )
    allowed = (query_id[:, None] == key_id[None, :]) & (key_token[None, :] <= query_token[:, None])
    scores = jnp.where(allowed[None], scores, -jnp.inf)
    row_max = jnp.max(scores, axis=-1, keepdims=True)
    raised = jnp.exp(scores - row_max)
    probs = (raised / jnp.sum(raised, axis=-1, keepdims=True)).astype(jnp.bfloat16)
    mixed = jnp.einsum("hqk,khd->qhd", probs, value_rows, preferred_element_type=jnp.float32)
    return mixed.astype(jnp.bfloat16)


def local(query_proj, key_proj, value_proj, lengths, page_table, out_weight, out_bias):
    local_heads = query_proj.shape[1] // DH
    device_rank = lax.axis_index(REQ)
    first_token = device_rank * TOK_DEV
    own_tokens = first_token + jnp.arange(TOK_DEV, dtype=jnp.int32)
    request_id, position = request_info(lengths, own_tokens)
    query_rot = rotate_heads(query_proj.reshape(TOK_DEV, local_heads, DH), position)
    key_flat = rotate_heads(key_proj.reshape(TOK_DEV, local_heads, DH), position).reshape(
        TOK_DEV, local_heads * DH
    )
    key_list = [key_flat]
    value_list = [value_proj]
    for distance in range(1, REACH + 1):
        far_key, far_value = passed_along((key_flat, value_proj), REQ, distance)
        key_list.append(far_key)
        value_list.append(far_value)
    key_stack = jnp.stack(key_list[::-1], axis=0)
    value_stack = jnp.stack(value_list[::-1], axis=0)
    key_rows = (REACH + 1) * TOK_DEV
    key_all = key_stack.reshape(key_rows, local_heads, DH)
    value_all = value_stack.reshape(key_rows, local_heads, DH)
    key_tokens = first_token - REACH * TOK_DEV + jnp.arange(key_rows, dtype=jnp.int32)
    key_id, key_position = request_info(lengths, key_tokens)
    mixed = attend_block(query_rot, key_all, value_all, request_id, own_tokens, key_id, key_tokens)
    heads_out = mixed.reshape(TOK_DEV, local_heads * DH)
    weight_rows = lax.all_gather(out_weight, "core", axis=0, tiled=True)
    weight_rows = lax.all_gather(weight_rows, "x", axis=0, tiled=True)
    weight_rows = lax.all_gather(weight_rows, "z", axis=0, tiled=True)
    heads_all = lax.all_gather(heads_out, "head", axis=1, tiled=True)
    summed = jnp.dot(heads_all, weight_rows, preferred_element_type=jnp.float32)
    attended = (summed + out_bias).astype(jnp.bfloat16)
    local_page = page_table - device_rank * BLK_DEV
    picker = (local_page[:, None] == jnp.arange(BLK_DEV, dtype=jnp.int32)[None, :]).astype(
        jnp.bfloat16
    )
    page_blocks = jnp.stack(
        [
            key_flat.reshape(BLK_DEV, PAGE, local_heads * DH),
            value_proj.reshape(BLK_DEV, PAGE, local_heads * DH),
        ],
        axis=1,
    )
    kv_pages = jnp.einsum(
        "bp,bctd->pctd", picker, page_blocks, preferred_element_type=jnp.float32
    ).astype(jnp.bfloat16)
    return (attended, kv_pages)


def solution(mesh):
    devices = mesh.devices
    cores = len({d.core_on_chip for d in devices.flat})
    columns = len({d.coords[0] for d in devices.flat})
    req_size, head_size = devices.shape
    split = Mesh(
        devices.reshape(req_size // (columns * cores), columns, cores, head_size),
        ("z", "x", "core", "head"),
    )
    placed = (
        P(REQ, "head"),
        P(REQ, "head"),
        P(REQ, "head"),
        P(),
        P(REQ),
        P(REQ, "head"),
        P("head"),
    )
    return jax.shard_map(
        local,
        mesh=split,
        in_specs=placed,
        out_specs=(P(REQ, "head"), P(REQ, None, None, "head")),
        check_vma=False,
    )
```

profile of v0, /device:TPU:2, one launch (start us, length us, event | category | flops | bytes accessed | tf_op | source)
XLA Modules:
  0.0 200.4 jit_solution(546849596047994481)
XLA Ops:
  7.2 0.0 copy-start.5
  7.2 0.0 all-gather.3.cloned.1.call-start
  7.2 1.1 copy.50
  8.4 0.7 copy.44
  9.1 0.1 reduce-window.9
  9.2 0.1 multiply_reduce_fusion
  9.4 0.1 fusion.12
  9.5 0.1 multiply_cosine_fusion
  9.6 0.1 copy.47
  9.7 0.1 copy.48
  9.8 0.2 copy.65
  10.0 0.2 copy.66
  10.2 0.0 copy-start.2
  10.2 0.0 copy-start.3
  10.3 0.1 multiply_subtract_fusion
  10.4 0.1 copy.53
  10.5 0.1 copy.54
  10.7 4.0 %collective-permute-start.4 = (bf16[256,512]{0,1:T(8,128)(2,1)S(1)}, bf16[256,512]{0,1:T(8,128)(2,1)S(1)}, u32[]{:S(2)}, u32[]{:S(2)}) collective-permute-start(bf16[256,512]{0,1:T(8,128)(2,1)S(1)} %bitcast.39), channel_id=1, source_target_pairs={{0,16},{4,20},{8,24},{12,28},{16,32},{20,36},{24,40},{28,44},{32,4... | collective-permute-start | bytes 786440 | tf_op jit(solution)/shard_map/ppermute | solution.py:20
  14.7 3.0 %collective-permute-start.5 = (bf16[256,512]{0,1:T(8,128)(2,1)S(1)}, bf16[256,512]{0,1:T(8,128)(2,1)}, u32[]{:S(2)}, u32[]{:S(2)}) collective-permute-start(bf16[256,512]{0,1:T(8,128)(2,1)S(1)} %bitcast.40), channel_id=1, source_target_pairs={{0,12},{4,16},{8,20},{12,24},{16,28},{20,32},{24,36},{28,40},{32,4... | collective-permute-start | bytes 786440 | tf_op jit(solution)/shard_map/ppermute | solution.py:20
  17.7 3.3 %collective-permute-start.6 = (bf16[256,512]{0,1:T(8,128)(2,1)S(1)}, bf16[256,512]{0,1:T(8,128)(2,1)}, u32[]{:S(2)}, u32[]{:S(2)}) collective-permute-start(bf16[256,512]{0,1:T(8,128)(2,1)S(1)} %bitcast.41), channel_id=1, source_target_pairs={{0,8},{4,12},{8,16},{12,20},{16,24},{20,28},{24,32},{28,36},{32,40... | collective-permute-start | bytes 786440 | tf_op jit(solution)/shard_map/ppermute | solution.py:20
  21.0 3.5 %collective-permute-start.7 = (bf16[256,512]{0,1:T(8,128)(2,1)S(1)}, bf16[256,512]{0,1:T(8,128)(2,1)}, u32[]{:S(2)}, u32[]{:S(2)}) collective-permute-start(bf16[256,512]{0,1:T(8,128)(2,1)S(1)} %bitcast.42), channel_id=1, source_target_pairs={{0,4},{4,8},{8,12},{12,16},{16,20},{20,24},{24,28},{28,32},{32,36}... | collective-permute-start | bytes 786440 | tf_op jit(solution)/shard_map/ppermute | solution.py:20
  24.6 4.4 %collective-permute-start = (bf16[256,512]{1,0:T(8,128)(2,1)S(1)}, bf16[256,512]{1,0:T(8,128)(2,1)S(1)}, u32[]{:S(2)}, u32[]{:S(2)}) collective-permute-start(bf16[256,512]{1,0:T(8,128)(2,1)S(1)} %copy-done.2), channel_id=1, source_target_pairs={{0,16},{4,20},{8,24},{12,28},{16,32},{20,36},{24,40},{28,44},{32,4... | collective-permute-start | bytes 786440 | tf_op jit(solution)/shard_map/ppermute | solution.py:20
  29.0 0.1 copy.45
  29.1 0.2 copy.46
  29.3 0.1 slice.27
  29.5 0.1 convert_reduce_fusion
  29.6 0.3 compare_and_fusion
  30.0 0.3 subtract_convert_fusion
  30.2 1.0 pad_maximum_fusion.2
  31.2 0.0 collective-permute-done.4
  31.2 2.1 %collective-permute-start.1 = (bf16[256,512]{1,0:T(8,128)(2,1)S(1)}, bf16[256,512]{1,0:T(8,128)(2,1)S(1)}, u32[]{:S(2)}, u32[]{:S(2)}) collective-permute-start(bf16[256,512]{1,0:T(8,128)(2,1)S(1)} %copy-done.2), channel_id=1, source_target_pairs={{0,12},{4,16},{8,20},{12,24},{16,28},{20,32},{24,36},{28,40},{32,4... | collective-permute-start | bytes 786440 | tf_op jit(solution)/shard_map/ppermute | solution.py:20
  33.3 0.7 bitcast_dynamic-update-slice_fusion.3
  34.0 0.6 collective-permute-done
  34.7 9.2 %collective-permute-start.2 = (bf16[256,512]{1,0:T(8,128)(2,1)S(1)}, bf16[256,512]{1,0:T(8,128)(2,1)}, u32[]{:S(2)}, u32[]{:S(2)}) collective-permute-start(bf16[256,512]{1,0:T(8,128)(2,1)S(1)} %copy-done.2), channel_id=1, source_target_pairs={{0,8},{4,12},{8,16},{12,20},{16,24},{20,28},{24,32},{28,36},{32,40... | collective-permute-start | bytes 786440 | tf_op jit(solution)/shard_map/ppermute | solution.py:20
  43.9 4.4 %collective-permute-start.3 = (bf16[256,512]{1,0:T(8,128)(2,1)S(1)}, bf16[256,512]{1,0:T(8,128)(2,1)}, u32[]{:S(2)}, u32[]{:S(2)}) collective-permute-start(bf16[256,512]{1,0:T(8,128)(2,1)S(1)} %copy-done.2), channel_id=1, source_target_pairs={{0,4},{4,8},{8,12},{12,16},{16,20},{20,24},{24,28},{28,32},{32,36}... | collective-permute-start | bytes 786440 | tf_op jit(solution)/shard_map/ppermute | solution.py:20
  48.2 1.7 bitcast_dynamic-update-slice_fusion.2
  49.9 1.7 bitcast_dynamic-update-slice_fusion.1
  51.6 1.7 bitcast_dynamic-update-slice_fusion
  53.2 0.0 collective-permute-done.1
  53.3 0.7 constant_dynamic-update-slice_fusion
  54.0 1.6 copy.55
  55.6 1.2 reshape.208
  56.8 1.0 bitcast_dynamic-update-slice_fusion.6
  57.8 0.0 collective-permute-done.3
  57.8 1.0 bitcast_dynamic-update-slice_fusion.5
  58.8 1.2 reshape.206
  60.1 0.5 copy-done
  60.6 3.1 %exponential_reduce_fusion = f32[4,256]{1,0:T(4,128)S(1)} fusion(bf16[256,4,128]{2,0,1:T(8,128)(2,1)} %pad_maximum_fusion.2, pred[256,1280]{1,0:T(8,128)(4,1)S(1)} %compare_and_fusion, bf16[1280,4,128]{2,1,0:T(4,128)(2,1)S(1)} %copy-done), kind=kOutput, calls=%fused_computation.4 | convolution fusion | flops 340788480 | bytes 1904640 | tf_op jit(solution)/shard_map/sub | solution.py:61
  63.7 0.0 copy-start.4
  63.7 4.5 %fusion.6 = bf16[4,128,256]{2,1,0:T(8,128)(2,1)} fusion(f32[4,256]{1,0:T(4,128)S(1)} %exponential_reduce_fusion, bf16[1280,4,128]{2,1,0:T(4,128)(2,1)S(1)} %copy-done.1, bf16[256,4,128]{2,0,1:T(8,128)(2,1)} %pad_maximum_fusion.2, pred[256,1280]{1,0:T(8,128)(4,1)S(1)} %compare_and_fusion, bf16[1280,4,128]{2,1,0:T(4,128)(2,1)S(1)} %copy-done), kind=kOutput, calls=%fused_computation.12 | convolution fusion | flops 677775616 | bytes 3477504 | tf_op jit(solution)/shard_map/hqk,khd->qhd/dot_general | solution.py:63
  68.2 0.0 all-gather.3.cloned.1.call-update
  68.2 0.0 all-gather.5.cloned.1.call-start
  68.2 3.1 %all_gather.13 = bf16[32,1024]{1,0:T(8,128)(2,1)S(1)} all-gather(bf16[16,1024]{1,0:T(8,128)(2,1)S(1)} %copy-done.4), channel_id=1, replica_groups=mesh['z'=16,'x'=4,'core'=2,'head'=4] {'core'}, dimensions={0}, use_global_device_ids=true | all-gather | bytes 98304 | tf_op jit(solution)/shard_map/all_gather | solution.py:92
  71.3 16.0 %all_gather.14 = bf16[128,1024]{1,0:T(8,128)(2,1)} all-gather(bf16[32,1024]{1,0:T(8,128)(2,1)S(1)} %all_gather.13), channel_id=1, replica_groups=mesh['z'=16,'x'=4,'core'=2,'head'=4] {'x'}, dimensions={0}, use_global_device_ids=true | all-gather | bytes 327680 | tf_op jit(solution)/shard_map/all_gather | solution.py:93
  87.4 0.0 all-gather.5.cloned.1.call-update
  87.4 0.1 reshape.212
  87.5 0.4 copy.59
  87.9 0.3 copy.60
  88.2 0.0 copy-start.6
  88.2 0.7 convolution_convert_fusion
  88.9 0.9 copy.61
  89.7 18.8 %all-gather.3.cloned.1.call-done = bf16[256,2048]{0,1:T(8,128)(2,1)} async-done(((bf16[256,512]{0,1:T(8,128)(2,1)}), bf16[256,2048]{0,1:T(8,128)(2,1)}) %all-gather.3.cloned.1.call-update) | async-done | bytes 1048592 | tf_op jit(solution)/shard_map/all_gather | solution.py:95
  108.5 80.5 %all-gather.5.cloned.1.call-done = bf16[2048,1024]{1,0:T(8,128)(2,1)} async-done(((bf16[128,1024]{1,0:T(8,128)(2,1)}), bf16[2048,1024]{1,0:T(8,128)(2,1)}) %all-gather.5.cloned.1.call-update) | async-done | bytes 4194320 | tf_op jit(solution)/shard_map/all_gather | solution.py:94
  189.0 4.6 %fusion.5 = bf16[256,1024]{1,0:T(8,128)(2,1)} fusion(bf16[256,2048]{0,1:T(8,128)(2,1)} %all-gather.3.cloned.1.call-done, bf16[2048,1024]{1,0:T(8,128)(2,1)} %all-gather.5.cloned.1.call-done, f32[1024]{0:T(1024)S(1)} %copy-done.6), kind=kOutput, calls=%fused_computation.10 | convolution fusion | flops 1074266112 | bytes 5771264 | tf_op jit(solution)/shard_map/dot_general | solution.py:96
  (29 shorter events, 0.2 us)
Async XLA Ops:
  7.2 2.2 %copy-start.5 = (s32[64]{0:T(128)S(1)}, s32[64]{0:T(128)}, u32[]{:S(2)}) copy-start(s32[64]{0:T(128)} %param.10) | copy-start | bytes 772
  7.2 101.3 %all-gather.3.cloned.1.call-start = ((), (), s32[]{:S(2)}) async-start(), calls=%async_computation | async-start | bytes 1310720 | tf_op jit(solution)/shard_map/all_gather | solution.py:95
  10.2 14.3 %copy-start.2 = (bf16[256,512]{1,0:T(8,128)(2,1)S(1)}, bf16[256,512]{1,0:T(8,128)(2,1)}, u32[]{:S(2)}) copy-start(bf16[256,512]{1,0:T(8,128)(2,1)} %param.9) | copy-start | bytes 786436
  10.2 18.7 %copy-start.3 = (bf16[256,512]{1,0:T(8,128)(2,1)S(1)}, bf16[256,512]{1,0:T(8,128)(2,1)}, u32[]{:S(2)}) copy-start(bf16[256,512]{1,0:T(8,128)(2,1)} %param.7) | copy-start | bytes 786436
  10.7 20.5 %collective-permute-start.4 = (bf16[256,512]{0,1:T(8,128)(2,1)S(1)}, bf16[256,512]{0,1:T(8,128)(2,1)S(1)}, u32[]{:S(2)}, u32[]{:S(2)}) collective-permute-start(bf16[256,512]{0,1:T(8,128)(2,1)S(1)} %bitcast.39), channel_id=1, source_target_pairs={{0,16},{4,20},{8,24},{12,28},{16,32},{20,36},{24,40},{28,44},{32,4... | collective-permute-start | bytes 786440 | tf_op jit(solution)/shard_map/ppermute | solution.py:20
  14.7 29.1 %collective-permute-start.5 = (bf16[256,512]{0,1:T(8,128)(2,1)S(1)}, bf16[256,512]{0,1:T(8,128)(2,1)}, u32[]{:S(2)}, u32[]{:S(2)}) collective-permute-start(bf16[256,512]{0,1:T(8,128)(2,1)S(1)} %bitcast.40), channel_id=1, source_target_pairs={{0,12},{4,16},{8,20},{12,24},{16,28},{20,32},{24,36},{28,40},{32,4... | collective-permute-start | bytes 786440 | tf_op jit(solution)/shard_map/ppermute | solution.py:20
  17.7 32.2 %collective-permute-start.6 = (bf16[256,512]{0,1:T(8,128)(2,1)S(1)}, bf16[256,512]{0,1:T(8,128)(2,1)}, u32[]{:S(2)}, u32[]{:S(2)}) collective-permute-start(bf16[256,512]{0,1:T(8,128)(2,1)S(1)} %bitcast.41), channel_id=1, source_target_pairs={{0,8},{4,12},{8,16},{12,20},{16,24},{20,28},{24,32},{28,36},{32,40... | collective-permute-start | bytes 786440 | tf_op jit(solution)/shard_map/ppermute | solution.py:20
  21.0 30.5 %collective-permute-start.7 = (bf16[256,512]{0,1:T(8,128)(2,1)S(1)}, bf16[256,512]{0,1:T(8,128)(2,1)}, u32[]{:S(2)}, u32[]{:S(2)}) collective-permute-start(bf16[256,512]{0,1:T(8,128)(2,1)S(1)} %bitcast.42), channel_id=1, source_target_pairs={{0,4},{4,8},{8,12},{12,16},{16,20},{20,24},{24,28},{28,32},{32,36}... | collective-permute-start | bytes 786440 | tf_op jit(solution)/shard_map/ppermute | solution.py:20
  24.6 10.1 %collective-permute-start = (bf16[256,512]{1,0:T(8,128)(2,1)S(1)}, bf16[256,512]{1,0:T(8,128)(2,1)S(1)}, u32[]{:S(2)}, u32[]{:S(2)}) collective-permute-start(bf16[256,512]{1,0:T(8,128)(2,1)S(1)} %copy-done.2), channel_id=1, source_target_pairs={{0,16},{4,20},{8,24},{12,28},{16,32},{20,36},{24,40},{28,44},{32,4... | collective-permute-start | bytes 786440 | tf_op jit(solution)/shard_map/ppermute | solution.py:20
  31.2 22.1 %collective-permute-start.1 = (bf16[256,512]{1,0:T(8,128)(2,1)S(1)}, bf16[256,512]{1,0:T(8,128)(2,1)S(1)}, u32[]{:S(2)}, u32[]{:S(2)}) collective-permute-start(bf16[256,512]{1,0:T(8,128)(2,1)S(1)} %copy-done.2), channel_id=1, source_target_pairs={{0,12},{4,16},{8,20},{12,24},{16,28},{20,32},{24,36},{28,40},{32,4... | collective-permute-start | bytes 786440 | tf_op jit(solution)/shard_map/ppermute | solution.py:20
  34.7 22.2 %collective-permute-start.2 = (bf16[256,512]{1,0:T(8,128)(2,1)S(1)}, bf16[256,512]{1,0:T(8,128)(2,1)}, u32[]{:S(2)}, u32[]{:S(2)}) collective-permute-start(bf16[256,512]{1,0:T(8,128)(2,1)S(1)} %copy-done.2), channel_id=1, source_target_pairs={{0,8},{4,12},{8,16},{12,20},{16,24},{20,28},{24,32},{28,36},{32,40... | collective-permute-start | bytes 786440 | tf_op jit(solution)/shard_map/ppermute | solution.py:20
  43.9 13.9 %collective-permute-start.3 = (bf16[256,512]{1,0:T(8,128)(2,1)S(1)}, bf16[256,512]{1,0:T(8,128)(2,1)}, u32[]{:S(2)}, u32[]{:S(2)}) collective-permute-start(bf16[256,512]{1,0:T(8,128)(2,1)S(1)} %copy-done.2), channel_id=1, source_target_pairs={{0,4},{4,8},{8,12},{12,16},{16,20},{20,24},{24,28},{28,32},{32,36}... | collective-permute-start | bytes 786440 | tf_op jit(solution)/shard_map/ppermute | solution.py:20
  58.8 1.8 copy-start
  60.6 3.1 %copy-start.1 = (bf16[1280,4,128]{2,1,0:T(4,128)(2,1)S(1)}, bf16[1280,4,128]{2,1,0:T(4,128)(2,1)}, u32[]{:S(2)}) copy-start(bf16[1280,4,128]{2,1,0:T(4,128)(2,1)} %reshape.206) | copy-start | bytes 3932164
  63.7 4.6 %copy-start.4 = (bf16[16,1024]{1,0:T(8,128)(2,1)S(1)}, bf16[16,1024]{1,0:T(8,128)(2,1)}, u32[]{:S(2)}) copy-start(bf16[16,1024]{1,0:T(8,128)(2,1)} %param.12) | copy-start | bytes 98308
  68.2 20.0 %copy-start.7 = (s32[2]{0:T(128)S(1)}, s32[2]{0:T(128)}, u32[]{:S(2)}) copy-start(s32[2]{0:T(128)} %param.11) | copy-start | bytes 28
  68.2 120.8 %all-gather.5.cloned.1.call-start = ((), (), s32[]{:S(2)}) async-start(), calls=%async_computation.1 | async-start | bytes 4456448 | tf_op jit(solution)/shard_map/all_gather | solution.py:94
  88.2 100.9 %copy-start.6 = (f32[1024]{0:T(1024)S(1)}, f32[1024]{0:T(1024)}, u32[]{:S(2)}) copy-start(f32[1024]{0:T(1024)} %param.13) | copy-start | bytes 12292
Sparse Core Ops, SparseCore 0:
  68.3 40.1 all-gather.2
  110.6 78.3 all-gather.4
where the time goes:
time: 201 us; the launch traced here: 200 us
  waiting for transfers between devices  100 us (50%)
  starting transfers between devices  34 us (17%)
  blocking collectives  19.1 us (10%)
  local copies, waits for them, and re-layouts  17.7 us (9%)
  between operations  14.5 us (7%)
  matrix products  12.8 us (6%)
  other arithmetic  2.33 us (1%)
    all_gather x1, waiting for transfers between devices, local(): weight_rows = lax.all_gather(weight_rows, 'z', axis=0, tiled=True)  80.5 us
    ppermute x8, starting transfers between devices, passed_along(): return lax.ppermute(array, axis, pairs)  33.9 us
    all_gather x1, waiting for transfers between devices, local(): heads_all = lax.all_gather(heads_out, 'head', axis=1, tiled=True)  18.8 us
    all_gather x1, blocking collectives, local(): weight_rows = lax.all_gather(weight_rows, 'x', axis=0, tiled=True)  16 us
    unnamed x29, local copies, waits for them, and re-layouts  10.7 us
    dot_general x1, matrix products, local(): summed = jnp.dot(heads_all, weight_rows, preferred_element_type=jnp.float32)  4.59 us
    dot_general x1, matrix products, attend_block(): jnp.einsum('hqk,khd->qhd', probs, value_rows, preferred_element_type=jnp....  4.48 us
  transfers between devices with their start and end apart: 10, of which 3 were waited for; matrix products, arithmetic and copies ran while one was open for 7% of the time, Pallas kernels for 0%

commit v1 on v0

--- a/solution.py
+++ b/solution.py
@@ -12,6 +12,28 @@
 TOK_DEV = 256
 rope_base = 10000.0
 REQ = ("z", "x", "core")
+
+
+def joined_along(blocks, dim):
+    blocks = jnp.moveaxis(blocks, 0, dim)
+    lengths = blocks.shape
+    return blocks.reshape(*lengths[:dim], lengths[dim] * lengths[dim + 1], *lengths[dim + 2 :])
+
+
+def ring_gather(shard, axis, dim):
+    devices = lax.axis_size(axis)
+    pairs = [(i, (i + 1) % devices) for i in range(devices)]
+    back = [(b, a) for a, b in pairs]
+    lower, upper = ([], [])
+    for turn in range(devices - 1):
+        if turn % 2 == 0:
+            lower.append(lax.ppermute(lower[-1] if lower else shard, axis, pairs))
+        else:
+            upper.append(lax.ppermute(upper[-1] if upper else shard, axis, back))
+    parts = jnp.stack([*lower[::-1], shard, *upper])
+    shift = lax.axis_index(axis) - len(lower)
+    parts = parts[(jnp.arange(devices) - shift) % devices]
+    return joined_along(parts, dim)
 
 
 def passed_along(array, axis, by):
@@ -92,7 +114,7 @@
     weight_rows = lax.all_gather(out_weight, "core", axis=0, tiled=True)
     weight_rows = lax.all_gather(weight_rows, "x", axis=0, tiled=True)
     weight_rows = lax.all_gather(weight_rows, "z", axis=0, tiled=True)
-    heads_all = lax.all_gather(heads_out, "head", axis=1, tiled=True)
+    heads_all = ring_gather(heads_out, "head", 1)
     summed = jnp.dot(heads_all, weight_rows, preferred_element_type=jnp.float32)
     attended = (summed + out_bias).astype(jnp.bfloat16)
     local_page = page_table - device_rank * BLK_DEV

time: 201 us -> 152 us (0.76)
  the two profiles are of different devices: /device:TPU:2 before, /device:TPU:256 now
where the time goes in v1:
time: 152 us; the launch traced here: 151 us
  starting transfers between devices  53.6 us (35%)
  waiting for transfers between devices  33.7 us (22%)
  local copies, waits for them, and re-layouts  18.4 us (12%)
  blocking collectives  15.5 us (10%)
  between operations  14.5 us (10%)
  matrix products  12.5 us (8%)
  other arithmetic  3.15 us (2%)
    ppermute x8, starting transfers between devices, passed_along(): return lax.ppermute(array, axis, pairs)  44.4 us
    ppermute x8, waiting for transfers between devices, passed_along(): return lax.ppermute(array, axis, pairs)  23 us
    all_gather x1, blocking collectives, local(): weight_rows = lax.all_gather(weight_rows, 'x', axis=0, tiled=True)  13.3 us
    unnamed x29, local copies, waits for them, and re-layouts  10.8 us
    ppermute x2, waiting for transfers between devices, ring_gather(): lower.append(lax.ppermute(lower[-1] if lower else shard, axis, pairs))  10.6 us
    ppermute x2, starting transfers between devices, ring_gather(): lower.append(lax.ppermute(lower[-1] if lower else shard, axis, pairs))  5.61 us
    dot_general x1, matrix products, attend_block(): jnp.einsum('hqk,khd->qhd', probs, value_rows, preferred_element_type=jnp....  4.48 us
    dot_general x1, matrix products, local(): summed = jnp.dot(heads_all, weight_rows, preferred_element_type=jnp.float32)  4.26 us
  transfers between devices with their start and end apart: 12, of which 4 were waited for; matrix products, arithmetic and copies ran while one was open for 19% of the time, Pallas kernels for 0%

profile of v1, /device:TPU:256, one launch (start us, length us, event | category | flops | bytes accessed | tf_op | source)
XLA Modules:
  0.0 151.4 jit_solution(139351428593524942)
XLA Ops:
  7.2 0.0 all-gather.2.cloned.1.call-start
  7.2 2.2 %all_gather.9 = bf16[32,1024]{1,0:T(8,128)(2,1)S(1)} all-gather(bf16[16,1024]{1,0:T(8,128)(2,1)} %param.12), channel_id=1, replica_groups=mesh['z'=16,'x'=4,'core'=2,'head'=4] {'core'}, dimensions={0}, use_global_device_ids=true | all-gather | bytes 98304 | tf_op jit(solution)/shard_map/all_gather | solution.py:114
  9.4 13.3 %all_gather.10 = bf16[128,1024]{1,0:T(8,128)(2,1)} all-gather(bf16[32,1024]{1,0:T(8,128)(2,1)S(1)} %all_gather.9), channel_id=1, replica_groups=mesh['z'=16,'x'=4,'core'=2,'head'=4] {'x'}, dimensions={0}, use_global_device_ids=true | all-gather | bytes 327680 | tf_op jit(solution)/shard_map/all_gather | solution.py:115
  22.8 0.0 all-gather.2.cloned.1.call-update
  22.8 0.7 copy.44
  23.5 0.1 reduce-window.9
  23.6 0.1 multiply_reduce_fusion
  23.8 0.7 multiply_subtract_fusion.1
  24.4 0.1 fusion.12
  24.5 0.1 multiply_cosine_fusion
  24.7 0.1 copy.47
  24.8 0.1 copy.48
  24.9 0.1 copy.50
  25.1 0.2 copy.65
  25.3 0.2 copy.66
  25.5 0.1 multiply_subtract_fusion
  25.7 0.1 copy.53
  25.8 0.1 copy.54
  25.9 3.4 %collective-permute-start.4 = (bf16[256,512]{0,1:T(8,128)(2,1)S(1)}, bf16[256,512]{0,1:T(8,128)(2,1)S(1)}, u32[]{:S(2)}, u32[]{:S(2)}) collective-permute-start(bf16[256,512]{0,1:T(8,128)(2,1)S(1)} %bitcast.49), channel_id=1, source_target_pairs={{0,16},{4,20},{8,24},{12,28},{16,32},{20,36},{24,40},{28,44},{32,4... | collective-permute-start | bytes 786440 | tf_op jit(solution)/shard_map/ppermute | solution.py:42
  29.3 1.9 %collective-permute-start.5 = (bf16[256,512]{0,1:T(8,128)(2,1)S(1)}, bf16[256,512]{0,1:T(8,128)(2,1)}, u32[]{:S(2)}, u32[]{:S(2)}) collective-permute-start(bf16[256,512]{0,1:T(8,128)(2,1)S(1)} %bitcast.50), channel_id=1, source_target_pairs={{0,12},{4,16},{8,20},{12,24},{16,28},{20,32},{24,36},{28,40},{32,4... | collective-permute-start | bytes 786440 | tf_op jit(solution)/shard_map/ppermute | solution.py:42
  31.2 3.8 %collective-permute-start.6 = (bf16[256,512]{0,1:T(8,128)(2,1)S(1)}, bf16[256,512]{0,1:T(8,128)(2,1)}, u32[]{:S(2)}, u32[]{:S(2)}) collective-permute-start(bf16[256,512]{0,1:T(8,128)(2,1)S(1)} %bitcast.51), channel_id=1, source_target_pairs={{0,8},{4,12},{8,16},{12,20},{16,24},{20,28},{24,32},{28,36},{32,40... | collective-permute-start | bytes 786440 | tf_op jit(solution)/shard_map/ppermute | solution.py:42
  35.1 3.7 %collective-permute-start.7 = (bf16[256,512]{0,1:T(8,128)(2,1)S(1)}, bf16[256,512]{0,1:T(8,128)(2,1)}, u32[]{:S(2)}, u32[]{:S(2)}) collective-permute-start(bf16[256,512]{0,1:T(8,128)(2,1)S(1)} %bitcast.52), channel_id=1, source_target_pairs={{0,4},{4,8},{8,12},{12,16},{16,20},{20,24},{24,28},{28,32},{32,36}... | collective-permute-start | bytes 786440 | tf_op jit(solution)/shard_map/ppermute | solution.py:42
  38.7 4.6 %collective-permute-start = (bf16[256,512]{1,0:T(8,128)(2,1)S(1)}, bf16[256,512]{1,0:T(8,128)(2,1)}, u32[]{:S(2)}, u32[]{:S(2)}) collective-permute-start(bf16[256,512]{1,0:T(8,128)(2,1)S(1)} %copy-done.2), channel_id=1, source_target_pairs={{0,16},{4,20},{8,24},{12,28},{16,32},{20,36},{24,40},{28,44},{32,4... | collective-permute-start | bytes 786440 | tf_op jit(solution)/shard_map/ppermute | solution.py:42
  43.3 0.1 copy.45
  43.5 0.2 copy.46
  43.7 0.1 slice.29
  43.9 0.1 convert_reduce_fusion
  44.0 0.3 compare_and_fusion
  44.3 0.3 subtract_convert_fusion
  44.6 1.0 pad_maximum_fusion.3
  45.6 1.9 %collective-permute-start.1 = (bf16[256,512]{1,0:T(8,128)(2,1)S(1)}, bf16[256,512]{1,0:T(8,128)(2,1)S(1)}, u32[]{:S(2)}, u32[]{:S(2)}) collective-permute-start(bf16[256,512]{1,0:T(8,128)(2,1)S(1)} %copy-done.2), channel_id=1, source_target_pairs={{0,12},{4,16},{8,20},{12,24},{16,28},{20,32},{24,36},{28,40},{32,4... | collective-permute-start | bytes 786440 | tf_op jit(solution)/shard_map/ppermute | solution.py:42
  47.5 0.7 bitcast_dynamic-update-slice_fusion.3
  48.2 10.3 %collective-permute-done = bf16[256,512]{1,0:T(8,128)(2,1)} collective-permute-done((bf16[256,512]{1,0:T(8,128)(2,1)S(1)}, bf16[256,512]{1,0:T(8,128)(2,1)}, u32[]{:S(2)}, u32[]{:S(2)}) %collective-permute-start) | collective-permute-done | bytes 262176 | tf_op jit(solution)/shard_map/ppermute | solution.py:42
  58.5 10.1 %collective-permute-start.2 = (bf16[256,512]{1,0:T(8,128)(2,1)S(1)}, bf16[256,512]{1,0:T(8,128)(2,1)}, u32[]{:S(2)}, u32[]{:S(2)}) collective-permute-start(bf16[256,512]{1,0:T(8,128)(2,1)S(1)} %copy-done.2), channel_id=1, source_target_pairs={{0,8},{4,12},{8,16},{12,20},{16,24},{20,28},{24,32},{28,36},{32,40... | collective-permute-start | bytes 786440 | tf_op jit(solution)/shard_map/ppermute | solution.py:42
  68.6 1.0 bitcast_dynamic-update-slice_fusion.8
  69.6 15.1 %collective-permute-start.3 = (bf16[256,512]{1,0:T(8,128)(2,1)S(1)}, bf16[256,512]{1,0:T(8,128)(2,1)}, u32[]{:S(2)}, u32[]{:S(2)}) collective-permute-start(bf16[256,512]{1,0:T(8,128)(2,1)S(1)} %copy-done.2), channel_id=1, source_target_pairs={{0,4},{4,8},{8,12},{12,16},{16,20},{20,24},{24,28},{28,32},{32,36}... | collective-permute-start | bytes 786440 | tf_op jit(solution)/shard_map/ppermute | solution.py:42
  84.7 1.7 %bitcast_dynamic-update-slice_fusion.2 = bf16[5,256,512]{1,2,0:T(8,128)(2,1)} fusion(bf16[5,256,512]{1,2,0:T(8,128)(2,1)} %bitcast_dynamic-update-slice_fusion.3, bf16[256,512]{0,1:T(8,128)(2,1)} %collective-permute-done.5), kind=kLoop, calls=%fused_computation.26 | loop fusion | bytes 524288
  86.4 1.7 %bitcast_dynamic-update-slice_fusion.1 = bf16[5,256,512]{1,2,0:T(8,128)(2,1)} fusion(bf16[5,256,512]{1,2,0:T(8,128)(2,1)} %bitcast_dynamic-update-slice_fusion.2, bf16[256,512]{0,1:T(8,128)(2,1)} %collective-permute-done.6), kind=kLoop, calls=%fused_computation.25 | loop fusion | bytes 524288
  88.0 1.7 %bitcast_dynamic-update-slice_fusion = bf16[5,256,512]{1,2,0:T(8,128)(2,1)} fusion(bf16[5,256,512]{1,2,0:T(8,128)(2,1)} %bitcast_dynamic-update-slice_fusion.1, bf16[256,512]{0,1:T(8,128)(2,1)} %collective-permute-done.7), kind=kLoop, calls=%fused_computation.24 | loop fusion | bytes 524288
  89.7 0.7 constant_dynamic-update-slice_fusion
  90.4 1.6 %copy.55 = bf16[5,256,512]{2,1,0:T(8,128)(2,1)S(1)} copy(bf16[5,256,512]{1,2,0:T(8,128)(2,1)} %constant_dynamic-update-slice_fusion) | data formatting | bytes 2621440 | tf_op jit(solution)/shard_map/stack | solution.py:105
  92.1 1.2 reshape.260
  93.3 1.0 bitcast_dynamic-update-slice_fusion.6
  94.3 12.7 %collective-permute-done.3 = bf16[256,512]{1,0:T(8,128)(2,1)} collective-permute-done((bf16[256,512]{1,0:T(8,128)(2,1)S(1)}, bf16[256,512]{1,0:T(8,128)(2,1)}, u32[]{:S(2)}, u32[]{:S(2)}) %collective-permute-start.3) | collective-permute-done | bytes 262176 | tf_op jit(solution)/shard_map/ppermute | solution.py:42
  107.0 1.0 bitcast_dynamic-update-slice_fusion.5
  108.0 1.3 reshape.258
  109.2 0.5 copy-done
  109.7 3.1 %exponential_reduce_fusion = f32[4,256]{1,0:T(4,128)S(1)} fusion(bf16[256,4,128]{2,0,1:T(8,128)(2,1)} %pad_maximum_fusion.3, pred[256,1280]{1,0:T(8,128)(4,1)S(1)} %compare_and_fusion, bf16[1280,4,128]{2,1,0:T(4,128)(2,1)S(1)} %copy-done), kind=kOutput, calls=%fused_computation.5 | convolution fusion | flops 340788480 | bytes 1904640 | tf_op jit(solution)/shard_map/sub | solution.py:83
  112.8 4.5 %fusion.6 = bf16[4,128,256]{2,1,0:T(8,128)(2,1)} fusion(f32[4,256]{1,0:T(4,128)S(1)} %exponential_reduce_fusion, bf16[1280,4,128]{2,1,0:T(4,128)(2,1)S(1)} %copy-done.1, bf16[256,4,128]{2,0,1:T(8,128)(2,1)} %pad_maximum_fusion.3, pred[256,1280]{1,0:T(8,128)(4,1)S(1)} %compare_and_fusion, bf16[1280,4,128]{2,1,0:T(4,128)(2,1)S(1)} %copy-done), kind=kOutput, calls=%fused_computation.13 | convolution fusion | flops 677775616 | bytes 3477504 | tf_op jit(solution)/shard_map/hqk,khd->qhd/dot_general | solution.py:85
  117.3 3.7 %collective-permute-start.8 = (bf16[256,512]{0,1:T(8,128)(2,1)}, bf16[256,512]{0,1:T(8,128)(2,1)S(1)}, u32[]{:S(2)}, u32[]{:S(2)}) collective-permute-start(bf16[256,512]{0,1:T(8,128)(2,1)} %bitcast.59), channel_id=1, source_target_pairs={{0,1},{1,2},{2,3},{3,0},{4,5},{5,6},{6,7},{7,4},{8,9},{9,10},{10,1... | collective-permute-start | bytes 786440 | tf_op jit(solution)/shard_map/ppermute | solution.py:30
  121.0 0.1 reshape.273
  121.1 0.4 copy.59
  121.5 0.3 copy.60
  121.8 3.5 %collective-permute-start.10 = (bf16[256,512]{0,1:T(8,128)(2,1)S(1)}, bf16[256,512]{0,1:T(8,128)(2,1)S(1)}, u32[]{:S(2)}, u32[]{:S(2)}) collective-permute-start(bf16[256,512]{0,1:T(8,128)(2,1)S(1)} %bitcast.60), channel_id=1, source_target_pairs={{1,0},{2,1},{3,2},{0,3},{5,4},{6,5},{7,6},{4,7},{9,8},{10,9},{11,1... | collective-permute-start | bytes 786440 | tf_op jit(solution)/shard_map/ppermute | solution.py:32
  125.3 4.6 %collective-permute-done.8 = bf16[256,512]{0,1:T(8,128)(2,1)S(1)} collective-permute-done((bf16[256,512]{0,1:T(8,128)(2,1)}, bf16[256,512]{0,1:T(8,128)(2,1)S(1)}, u32[]{:S(2)}, u32[]{:S(2)}) %collective-permute-start.8) | collective-permute-done | bytes 262176 | tf_op jit(solution)/shard_map/ppermute | solution.py:30
  130.0 1.9 %collective-permute-start.9 = (bf16[256,512]{0,1:T(8,128)(2,1)S(1)}, bf16[256,512]{0,1:T(8,128)(2,1)S(1)}, u32[]{:S(2)}, u32[]{:S(2)}) collective-permute-start(bf16[256,512]{0,1:T(8,128)(2,1)S(1)} %collective-permute-done.8), channel_id=1, source_target_pairs={{0,1},{1,2},{2,3},{3,0},{4,5},{5,6},{6,7},{7,4},{8,9},{9,10},{10,1... | collective-permute-start | bytes 786440 | tf_op jit(solution)/shard_map/ppermute | solution.py:30
  131.9 0.7 convolution_convert_fusion
  132.6 0.9 copy.61
  133.5 6.0 %collective-permute-done.9 = bf16[256,512]{0,1:T(8,128)(2,1)S(1)} collective-permute-done((bf16[256,512]{0,1:T(8,128)(2,1)S(1)}, bf16[256,512]{0,1:T(8,128)(2,1)S(1)}, u32[]{:S(2)}, u32[]{:S(2)}) %collective-permute-start.9) | collective-permute-done | bytes 262176 | tf_op jit(solution)/shard_map/ppermute | solution.py:30
  139.4 0.1 pad_maximum_fusion
  139.6 0.6 gather_fusion
  140.2 0.0 all-gather.2.cloned.1.call-done
  140.2 0.0 copy-done.6
  140.3 4.3 %fusion.5 = bf16[256,1024]{1,0:T(8,128)(2,1)} fusion(bf16[256,2048]{0,1:T(8,128)(2,1)S(1)} %bitcast.56, bf16[2048,1024]{1,0:T(8,128)(2,1)} %all-gather.2.cloned.1.call-done, f32[1024]{0:T(1024)S(1)} %copy-done.6), kind=kOutput, calls=%fused_computation.11 | convolution fusion | flops 1074266112 | bytes 5771264 | tf_op jit(solution)/shard_map/dot_general | solution.py:118
  (36 shorter events, 0.2 us)
Async XLA Ops:
  7.2 17.7 %copy-start.3 = (bf16[256,512]{1,0:T(8,128)(2,1)S(1)}, bf16[256,512]{1,0:T(8,128)(2,1)}, u32[]{:S(2)}) copy-start(bf16[256,512]{1,0:T(8,128)(2,1)} %param.8) | copy-start | bytes 786436
  7.2 133.1 %all-gather.2.cloned.1.call-start = ((), (), s32[]{:S(2)}) async-start(), calls=%async_computation | async-start | bytes 4456448 | tf_op jit(solution)/shard_map/all_gather | solution.py:116
  25.5 13.3 %copy-start.2 = (bf16[256,512]{1,0:T(8,128)(2,1)S(1)}, bf16[256,512]{1,0:T(8,128)(2,1)}, u32[]{:S(2)}) copy-start(bf16[256,512]{1,0:T(8,128)(2,1)} %param.9) | copy-start | bytes 786436
  25.5 17.8 %copy-start.4 = (bf16[256,512]{1,0:T(8,128)(2,1)S(1)}, bf16[256,512]{1,0:T(8,128)(2,1)}, u32[]{:S(2)}) copy-start(bf16[256,512]{1,0:T(8,128)(2,1)} %param.7) | copy-start | bytes 786436
  25.9 19.6 %collective-permute-start.4 = (bf16[256,512]{0,1:T(8,128)(2,1)S(1)}, bf16[256,512]{0,1:T(8,128)(2,1)S(1)}, u32[]{:S(2)}, u32[]{:S(2)}) collective-permute-start(bf16[256,512]{0,1:T(8,128)(2,1)S(1)} %bitcast.49), channel_id=1, source_target_pairs={{0,16},{4,20},{8,24},{12,28},{16,32},{20,36},{24,40},{28,44},{32,4... | collective-permute-start | bytes 786440 | tf_op jit(solution)/shard_map/ppermute | solution.py:42
  29.3 40.3 %collective-permute-start.5 = (bf16[256,512]{0,1:T(8,128)(2,1)S(1)}, bf16[256,512]{0,1:T(8,128)(2,1)}, u32[]{:S(2)}, u32[]{:S(2)}) collective-permute-start(bf16[256,512]{0,1:T(8,128)(2,1)S(1)} %bitcast.50), channel_id=1, source_target_pairs={{0,12},{4,16},{8,20},{12,24},{16,28},{20,32},{24,36},{28,40},{32,4... | collective-permute-start | bytes 786440 | tf_op jit(solution)/shard_map/ppermute | solution.py:42
  31.2 55.1 %collective-permute-start.6 = (bf16[256,512]{0,1:T(8,128)(2,1)S(1)}, bf16[256,512]{0,1:T(8,128)(2,1)}, u32[]{:S(2)}, u32[]{:S(2)}) collective-permute-start(bf16[256,512]{0,1:T(8,128)(2,1)S(1)} %bitcast.51), channel_id=1, source_target_pairs={{0,8},{4,12},{8,16},{12,20},{16,24},{20,28},{24,32},{28,36},{32,40... | collective-permute-start | bytes 786440 | tf_op jit(solution)/shard_map/ppermute | solution.py:42
  35.1 53.0 %collective-permute-start.7 = (bf16[256,512]{0,1:T(8,128)(2,1)S(1)}, bf16[256,512]{0,1:T(8,128)(2,1)}, u32[]{:S(2)}, u32[]{:S(2)}) collective-permute-start(bf16[256,512]{0,1:T(8,128)(2,1)S(1)} %bitcast.52), channel_id=1, source_target_pairs={{0,4},{4,8},{8,12},{12,16},{16,20},{20,24},{24,28},{28,32},{32,36}... | collective-permute-start | bytes 786440 | tf_op jit(solution)/shard_map/ppermute | solution.py:42
  38.7 19.8 %collective-permute-start = (bf16[256,512]{1,0:T(8,128)(2,1)S(1)}, bf16[256,512]{1,0:T(8,128)(2,1)}, u32[]{:S(2)}, u32[]{:S(2)}) collective-permute-start(bf16[256,512]{1,0:T(8,128)(2,1)S(1)} %copy-done.2), channel_id=1, source_target_pairs={{0,16},{4,20},{8,24},{12,28},{16,32},{20,36},{24,40},{28,44},{32,4... | collective-permute-start | bytes 786440 | tf_op jit(solution)/shard_map/ppermute | solution.py:42
  45.6 44.2 %collective-permute-start.1 = (bf16[256,512]{1,0:T(8,128)(2,1)S(1)}, bf16[256,512]{1,0:T(8,128)(2,1)S(1)}, u32[]{:S(2)}, u32[]{:S(2)}) collective-permute-start(bf16[256,512]{1,0:T(8,128)(2,1)S(1)} %copy-done.2), channel_id=1, source_target_pairs={{0,12},{4,16},{8,20},{12,24},{16,28},{20,32},{24,36},{28,40},{32,4... | collective-permute-start | bytes 786440 | tf_op jit(solution)/shard_map/ppermute | solution.py:42
  58.5 34.8 %collective-permute-start.2 = (bf16[256,512]{1,0:T(8,128)(2,1)S(1)}, bf16[256,512]{1,0:T(8,128)(2,1)}, u32[]{:S(2)}, u32[]{:S(2)}) collective-permute-start(bf16[256,512]{1,0:T(8,128)(2,1)S(1)} %copy-done.2), channel_id=1, source_target_pairs={{0,8},{4,12},{8,16},{12,20},{16,24},{20,28},{24,32},{28,36},{32,40... | collective-permute-start | bytes 786440 | tf_op jit(solution)/shard_map/ppermute | solution.py:42
  69.6 37.4 %collective-permute-start.3 = (bf16[256,512]{1,0:T(8,128)(2,1)S(1)}, bf16[256,512]{1,0:T(8,128)(2,1)}, u32[]{:S(2)}, u32[]{:S(2)}) collective-permute-start(bf16[256,512]{1,0:T(8,128)(2,1)S(1)} %copy-done.2), channel_id=1, source_target_pairs={{0,4},{4,8},{8,12},{12,16},{16,20},{20,24},{24,28},{28,32},{32,36}... | collective-permute-start | bytes 786440 | tf_op jit(solution)/shard_map/ppermute | solution.py:42
  108.0 1.8 %copy-start = (bf16[1280,4,128]{2,1,0:T(4,128)(2,1)S(1)}, bf16[1280,4,128]{2,1,0:T(4,128)(2,1)}, u32[]{:S(2)}) copy-start(bf16[1280,4,128]{2,1,0:T(4,128)(2,1)} %reshape.260) | copy-start | bytes 3932164
  109.7 3.1 %copy-start.1 = (bf16[1280,4,128]{2,1,0:T(4,128)(2,1)S(1)}, bf16[1280,4,128]{2,1,0:T(4,128)(2,1)}, u32[]{:S(2)}) copy-start(bf16[1280,4,128]{2,1,0:T(4,128)(2,1)} %reshape.258) | copy-start | bytes 3932164
  117.3 4.5 %copy-start.7 = (s32[2]{0:T(128)S(1)}, s32[2]{0:T(128)}, u32[]{:S(2)}) copy-start(s32[2]{0:T(128)} %param.11) | copy-start | bytes 28
  117.3 4.5 %copy-start.5 = (bf16[4,128,256]{2,1,0:T(8,128)(2,1)S(1)}, bf16[4,128,256]{2,1,0:T(8,128)(2,1)}, u32[]{:S(2)}) copy-start(bf16[4,128,256]{2,1,0:T(8,128)(2,1)} %fusion.6) | copy-start | bytes 786436
  117.3 12.7 %collective-permute-start.8 = (bf16[256,512]{0,1:T(8,128)(2,1)}, bf16[256,512]{0,1:T(8,128)(2,1)S(1)}, u32[]{:S(2)}, u32[]{:S(2)}) collective-permute-start(bf16[256,512]{0,1:T(8,128)(2,1)} %bitcast.59), channel_id=1, source_target_pairs={{0,1},{1,2},{2,3},{3,0},{4,5},{5,6},{6,7},{7,4},{8,9},{9,10},{10,1... | collective-permute-start | bytes 786440 | tf_op jit(solution)/shard_map/ppermute | solution.py:30
  121.8 11.7 %collective-permute-start.10 = (bf16[256,512]{0,1:T(8,128)(2,1)S(1)}, bf16[256,512]{0,1:T(8,128)(2,1)S(1)}, u32[]{:S(2)}, u32[]{:S(2)}) collective-permute-start(bf16[256,512]{0,1:T(8,128)(2,1)S(1)} %bitcast.60), channel_id=1, source_target_pairs={{1,0},{2,1},{3,2},{0,3},{5,4},{6,5},{7,6},{4,7},{9,8},{10,9},{11,1... | collective-permute-start | bytes 786440 | tf_op jit(solution)/shard_map/ppermute | solution.py:32
  130.0 9.5 %collective-permute-start.9 = (bf16[256,512]{0,1:T(8,128)(2,1)S(1)}, bf16[256,512]{0,1:T(8,128)(2,1)S(1)}, u32[]{:S(2)}, u32[]{:S(2)}) collective-permute-start(bf16[256,512]{0,1:T(8,128)(2,1)S(1)} %collective-permute-done.8), channel_id=1, source_target_pairs={{0,1},{1,2},{2,3},{3,0},{4,5},{5,6},{6,7},{7,4},{8,9},{9,10},{10,1... | collective-permute-start | bytes 786440 | tf_op jit(solution)/shard_map/ppermute | solution.py:30
  139.6 0.7 copy-start.6
Sparse Core Ops, SparseCore 0:
  22.9 73.9 all-gather.1
